TPU v7x, 32 devices: a whole 2x2x4 slice. The times are simulated.
32 devices in a mesh: elem: 8 (over z, x), cuts: 4 (over y, core).
Axes of the slice: x: 2, y: 2, z: 4, core: 2. Of those that a mesh axis runs over, the one named last changes fastest.
Arguments:
- basis: bfloat16 [8, 32768, 160], P('elem', 'cuts'), may hold values from -6 to 6
- quad_weight: float32 [8, 32768], P('elem', 'cuts'), may hold values from 0.5 to 2
- projectors: bfloat16 [8, 3, 20, 16, 32768], P('elem', None, None, None, 'cuts'), may hold values from -0.03125 to 0.03125
- species: int32 [8, 20], P('elem'), may hold values from 0 to 3
- counts: int32 [8, 20], P('elem'), may hold values from 1 to 16
- gamma_table: float32 [4, 16], replicated, may hold values from -0.4375 to 0.4375
Outputs:
- blocks: float32 [8, 3, 160, 160], P(None, None, 'elem', 'cuts')
Inputs may be any that keep to these rules, and one draw needn't show every extreme that they name: `counts`: each atom has at least one projector and at most 16.
All inputs are finite; a program needn't handle non-finite values.
Results may differ from a plain program's by a relative error of at most 0.004.
Values sent between devices are 32-bit elements; how exact they have to be, the bound alone decides.
No kernel may reach another device: no remote copies, remote signals or barrier semaphores. Data moves between devices by JAX's collectives and lax.ppermute only.
A program may use at most 64 MiB of HBM per device.

v0:
```python
import jax
import jax.numpy as jnp
from jax import lax
from jax.sharding import PartitionSpec as P


def passed_along(block, axis, distance):
    devices = range(lax.axis_size(axis))
    route = [((i - distance) % len(devices), i) for i in devices]
    return lax.ppermute(block, axis, route)


def pair_block(left, weights, right):
    return jnp.einsum("ib,ic->bc", left * weights[:, None], right, precision=lax.Precision.HIGHEST)


def local(basis, quad_weight, projectors, species, counts, gamma_table):
    width = basis.shape[2]
    groups, atoms, slots, points = projectors.shape[1:]
    span = atoms * slots
    quarter = width // lax.axis_size("cuts")
    cut_index = lax.axis_index("cuts")
    scaled = (basis[0].astype(jnp.float32) * quad_weight[0][:, None]).astype(jnp.bfloat16)
    partial_value = jnp.dot(
        projectors[0].reshape(groups * span, points), scaled, preferred_element_type=jnp.float32
    )
    onehot = (
        species[0][:, None] == jnp.arange(gamma_table.shape[0], dtype=jnp.int32)[None, :]
    ).astype(jnp.float32)
    table = jnp.dot(onehot, gamma_table, precision=lax.Precision.HIGHEST)
    active = (jnp.arange(slots, dtype=jnp.int32)[None, :] < counts[0][:, None]).astype(jnp.float32)
    energy = (table * active).reshape(span)
    full = lax.psum(partial_value, "cuts")
    left_whole, left_energy = passed_along((full[span:], energy), "elem", 1)
    right_whole, right_energy = passed_along((full[: 2 * span], energy), "elem", -1)
    start = cut_index * quarter
    own_share = lax.dynamic_slice_in_dim(full, start, quarter, 1)
    left_coef = lax.dynamic_slice_in_dim(left_whole, start, quarter, 1)
    right_coef = lax.dynamic_slice_in_dim(right_whole, start, quarter, 1)
    group0, group1, group2 = (full[:span], full[span : 2 * span], full[2 * span :])
    share0, share1, share2 = (own_share[:span], own_share[span : 2 * span], own_share[2 * span :])
    block_left = pair_block(group0, left_energy, left_coef[:span]) + pair_block(
        group1, energy, left_coef[span:]
    )
    block_diag = (
        pair_block(group0, left_energy, share0)
        + pair_block(group1, energy, share1)
        + pair_block(group2, right_energy, share2)
    )
    block_right = pair_block(group1, energy, right_coef[:span]) + pair_block(
        group2, right_energy, right_coef[span:]
    )
    stacked = jnp.stack([block_left, block_diag, block_right], axis=0)[None]
    return lax.all_to_all(stacked, "elem", split_axis=2, concat_axis=0, tiled=True)


def solution(mesh):
    in_specs = (
        P("elem", "cuts", None),
        P("elem", "cuts"),
        P("elem", None, None, None, "cuts"),
        P("elem", None),
        P("elem", None),
        P(),
    )
    out_specs = P(None, None, "elem", "cuts")
    return jax.shard_map(local, mesh=mesh, in_specs=in_specs, out_specs=out_specs, check_vma=False)
```

profile of v0, /device:TPU:0, one launch (start us, length us, event | category | flops | bytes accessed | tf_op | source)
XLA Modules:
  0.0 105.4 jit_solution(16012741648585391315)
XLA Ops:
  6.5 12.2 %fusion.4 = f32[960,160]{0,1:T(8,128)} fusion(bf16[960,8192]{1,0:T(8,128)(2,1)} %bitcast.32, bf16[1,8192,160]{1,2,0:T(8,128)(2,1)} %param.6, f32[8192]{0:T(1024)} %bitcast.33), kind=kOutput, calls=%fused_computation.4 | convolution fusion | flops 2520514560 | bytes 18997248 | tf_op jit(solution)/shard_map/dot_general | solution.py:24
  18.8 0.2 convolution_select_fusion
  19.1 2.9 %collective-permute-start = (f32[320]{0:T(512)S(1)}, f32[320]{0:T(512)S(1)}, u32[]{:S(2)}, u32[]{:S(2)}) collective-permute-start(f32[320]{0:T(512)S(1)} %reshape.16), channel_id=1, source_target_pairs={{28,0},{0,4},{4,8},{8,12},{12,16},{16,20},{20,24},{24,28},{29,1},{... | collective-permute-start | bytes 3848 | tf_op jit(solution)/shard_map/ppermute | solution.py:10
  22.1 3.1 %collective-permute-start.2 = (f32[320]{0:T(512)S(1)}, f32[320]{0:T(512)S(1)}, u32[]{:S(2)}, u32[]{:S(2)}) collective-permute-start(f32[320]{0:T(512)S(1)} %reshape.16), channel_id=1, source_target_pairs={{4,0},{8,4},{12,8},{16,12},{20,16},{24,20},{28,24},{0,28},{5,1},{9... | collective-permute-start | bytes 3848 | tf_op jit(solution)/shard_map/ppermute | solution.py:10
  25.2 30.2 %all-reduce.2.cloned.1.call-done = f32[960,160]{0,1:T(8,128)} async-done(((f32[960,160]{0,1:T(8,128)}), f32[960,160]{0,1:T(8,128)}) %all-reduce.2.cloned.1.call-update) | async-done | bytes 614416 | tf_op jit(solution)/shard_map/psum | solution.py:33
  55.4 1.4 %fusion.33 = (f32[640,160]{0,1:T(8,128)S(1)}, f32[640,160]{0,1:T(8,128)S(1)}) fusion(f32[960,160]{0,1:T(8,128)} %all-reduce.2.cloned.1.call-done), kind=kLoop, calls=%fused_computation.42 | loop fusion | bytes 1638400 | tf_op jit(solution)/shard_map/slice | solution.py:34
  56.8 1.5 %collective-permute-start.1 = (f32[640,160]{0,1:T(8,128)S(1)}, f32[640,160]{0,1:T(8,128)S(1)}, u32[]{:S(2)}, u32[]{:S(2)}) collective-permute-start(f32[640,160]{0,1:T(8,128)S(1)} %get-tuple-element.5), channel_id=1, source_target_pairs={{28,0},{0,4},{4,8},{8,12},{12,16},{16,20},{20,24},{24,28},{29,1},{... | collective-permute-start | bytes 1228808 | tf_op jit(solution)/shard_map/ppermute | solution.py:10
  58.3 3.3 %collective-permute-start.3 = (f32[640,160]{0,1:T(8,128)S(1)}, f32[640,160]{0,1:T(8,128)S(1)}, u32[]{:S(2)}, u32[]{:S(2)}) collective-permute-start(f32[640,160]{0,1:T(8,128)S(1)} %get-tuple-element.6), channel_id=1, source_target_pairs={{4,0},{8,4},{12,8},{16,12},{20,16},{24,20},{28,24},{0,28},{5,1},{9... | collective-permute-start | bytes 1228808 | tf_op jit(solution)/shard_map/ppermute | solution.py:10
  61.5 1.5 %fusion.13 = f32[160,40]{0,1:T(8,128)S(1)} fusion(f32[960,160]{0,1:T(8,128)} %all-reduce.2.cloned.1.call-done, f32[320]{0:T(512)S(1)} %reshape.16, s32[]{:T(128)S(6)} %add.24, s32[]{:T(128)S(6)} %select_n.2), kind=kOutput, calls=%fused_computation.19 | convolution fusion | flops 24627200 | bytes 334088 | tf_op jit(solution)/shard_map/ib,ic->bc/dot_general | solution.py:14
  63.0 1.4 %fusion.12 = f32[160,40]{0,1:T(8,128)S(1)} fusion(f32[960,160]{0,1:T(8,128)} %all-reduce.2.cloned.1.call-done, f32[320]{0:T(512)S(1)} %collective-permute-done.2, s32[]{:T(128)S(6)} %add.26, s32[]{:T(128)S(6)} %select_n.2), kind=kOutput, calls=%fused_computation.18 | convolution fusion | flops 24627200 | bytes 334088 | tf_op jit(solution)/shard_map/ib,ic->bc/dot_general | solution.py:14
  64.4 1.4 %fusion.10 = f32[1,160,40]{1,2,0:T(8,128)S(1)} fusion(f32[160,40]{0,1:T(8,128)S(1)} %fusion.12, f32[160,40]{0,1:T(8,128)S(1)} %fusion.13, f32[960,160]{0,1:T(8,128)} %all-reduce.2.cloned.1.call-done, f32[320]{0:T(512)S(1)} %collective-permute-done, s32[]{:T(128)S(6)} %select_n.2), kind=kOutput, calls=%fused_computation.11 | convolution fusion | flops 24640000 | bytes 385284 | tf_op jit(solution)/shard_map/ib,ic->bc/dot_general | solution.py:14
  65.8 9.1 %collective-permute-done.1 = f32[640,160]{0,1:T(8,128)S(1)} collective-permute-done((f32[640,160]{0,1:T(8,128)S(1)}, f32[640,160]{0,1:T(8,128)S(1)}, u32[]{:S(2)}, u32[]{:S(2)}) %collective-permute-start.1) | collective-permute-done | bytes 409632 | tf_op jit(solution)/shard_map/ppermute | solution.py:10
  74.9 1.5 %fusion.14 = f32[160,40]{0,1:T(8,128)S(1)} fusion(f32[960,160]{0,1:T(8,128)} %all-reduce.2.cloned.1.call-done, f32[320]{0:T(512)S(1)} %reshape.16, f32[640,160]{0,1:T(8,128)S(1)} %collective-permute-done.1, s32[]{:T(128)S(6)} %add.24, s32[]{:T(128)S(6)} %select_n.2), kind=kOutput, calls=%fused_computation.20 | convolution fusion | flops 24627200 | bytes 334856 | tf_op jit(solution)/shard_map/ib,ic->bc/dot_general | solution.py:14
  76.3 1.4 %fusion.8 = f32[1,160,40]{1,2,0:T(8,128)S(1)} fusion(f32[160,40]{0,1:T(8,128)S(1)} %fusion.14, f32[960,160]{0,1:T(8,128)} %all-reduce.2.cloned.1.call-done, f32[320]{0:T(512)S(1)} %collective-permute-done, f32[640,160]{0,1:T(8,128)S(1)} %collective-permute-done.1, s32[]{:T(128)S(6)} %select_n.2), kind=kOutput, calls=%fused_computation.9 | convolution fusion | flops 24633600 | bytes 375812 | tf_op jit(solution)/shard_map/ib,ic->bc/dot_general | solution.py:14
  77.7 1.4 %fusion.11 = f32[160,40]{0,1:T(8,128)S(1)} fusion(f32[960,160]{0,1:T(8,128)} %all-reduce.2.cloned.1.call-done, f32[320]{0:T(512)S(1)} %collective-permute-done.2, f32[640,160]{0,1:T(8,128)S(1)} %collective-permute-done.3, s32[]{:T(128)S(6)} %add.24, s32[]{:T(128)S(6)} %select_n.2), kind=kOutput, calls=%fused_computation.17 | convolution fusion | flops 24627200 | bytes 334856 | tf_op jit(solution)/shard_map/ib,ic->bc/dot_general | solution.py:14
  79.1 1.5 %fusion.7 = f32[1,160,40]{1,2,0:T(8,128)S(1)} fusion(f32[160,40]{0,1:T(8,128)S(1)} %fusion.11, f32[960,160]{0,1:T(8,128)} %all-reduce.2.cloned.1.call-done, f32[320]{0:T(512)S(1)} %reshape.16, f32[640,160]{0,1:T(8,128)S(1)} %collective-permute-done.3, s32[]{:T(128)S(6)} %select_n.2), kind=kOutput, calls=%fused_computation.6 | convolution fusion | flops 24633600 | bytes 375812 | tf_op jit(solution)/shard_map/ib,ic->bc/dot_general | solution.py:14
  80.8 0.5 broadcast.11
  81.3 1.4 %reduce = f32[160,3,40]{2,1,0:T(4,128)S(1)} reduce(f32[160,3,1,40]{3,2,1,0:T(1,128)S(1)} %bitcast.31, f32[]{:T(128)} %broadcast.11), dimensions={2}, to_apply=%bitcast.24.reduce_sub_computation | reduce | bytes 153604
  82.8 0.3 reshape.17
  83.1 13.3 %all_to_all.18 = f32[8,1,2400]{2,1,0:T(1,128)S(1)} all-to-all(f32[8,1,2400]{2,1,0:T(1,128)S(1)} %reshape.17), channel_id=1, replica_groups=mesh['elem'=8,'cuts'=4] {'elem'}, dimensions={0} | all-to-all | bytes 153600 | tf_op jit(solution)/shard_map/all_to_all | solution.py:54
  96.4 0.8 reduce.1
  97.2 0.5 reshape.18
  97.7 0.2 copy.20
  97.9 0.7 copy.23
  (15 shorter events, 0.4 us)
Async XLA Ops:
  6.5 12.2 %copy-start = (f32[4,16]{1,0:T(4,128)S(1)}, f32[4,16]{1,0:T(4,128)}, u32[]{:S(2)}) copy-start(f32[4,16]{1,0:T(4,128)} %param.11) | copy-start | bytes 772
  6.5 48.9 %all-reduce.2.cloned.1.call-start = ((), (), s32[]{:S(2)}) async-start(), calls=%async_computation.1 | async-start | bytes 1310720 | tf_op jit(solution)/shard_map/psum | solution.py:33
  6.5 12.2 %copy-start.1 = (s32[1,20]{1,0:T(1,128)S(1)}, s32[1,20]{1,0:T(1,128)}, u32[]{:S(2)}) copy-start(s32[1,20]{1,0:T(1,128)} %param.9) | copy-start | bytes 244
  6.5 12.2 %copy-start.2 = (s32[1,20]{1,0:T(1,128)S(1)}, s32[1,20]{1,0:T(1,128)}, u32[]{:S(2)}) copy-start(s32[1,20]{1,0:T(1,128)} %param.10) | copy-start | bytes 244
  19.1 45.3 %collective-permute-start = (f32[320]{0:T(512)S(1)}, f32[320]{0:T(512)S(1)}, u32[]{:S(2)}, u32[]{:S(2)}) collective-permute-start(f32[320]{0:T(512)S(1)} %reshape.16), channel_id=1, source_target_pairs={{28,0},{0,4},{4,8},{8,12},{12,16},{16,20},{20,24},{24,28},{29,1},{... | collective-permute-start | bytes 3848 | tf_op jit(solution)/shard_map/ppermute | solution.py:10
  22.1 40.9 %collective-permute-start.2 = (f32[320]{0:T(512)S(1)}, f32[320]{0:T(512)S(1)}, u32[]{:S(2)}, u32[]{:S(2)}) collective-permute-start(f32[320]{0:T(512)S(1)} %reshape.16), channel_id=1, source_target_pairs={{4,0},{8,4},{12,8},{16,12},{20,16},{24,20},{28,24},{0,28},{5,1},{9... | collective-permute-start | bytes 3848 | tf_op jit(solution)/shard_map/ppermute | solution.py:10
  56.8 18.1 %collective-permute-start.1 = (f32[640,160]{0,1:T(8,128)S(1)}, f32[640,160]{0,1:T(8,128)S(1)}, u32[]{:S(2)}, u32[]{:S(2)}) collective-permute-start(f32[640,160]{0,1:T(8,128)S(1)} %get-tuple-element.5), channel_id=1, source_target_pairs={{28,0},{0,4},{4,8},{8,12},{12,16},{16,20},{20,24},{24,28},{29,1},{... | collective-permute-start | bytes 1228808 | tf_op jit(solution)/shard_map/ppermute | solution.py:10
  58.3 19.4 %collective-permute-start.3 = (f32[640,160]{0,1:T(8,128)S(1)}, f32[640,160]{0,1:T(8,128)S(1)}, u32[]{:S(2)}, u32[]{:S(2)}) collective-permute-start(f32[640,160]{0,1:T(8,128)S(1)} %get-tuple-element.6), channel_id=1, source_target_pairs={{4,0},{8,4},{12,8},{16,12},{20,16},{24,20},{28,24},{0,28},{5,1},{9... | collective-permute-start | bytes 1228808 | tf_op jit(solution)/shard_map/ppermute | solution.py:10
Sparse Core Ops, SparseCore 0:
  18.9 36.5 all-reduce.1
where the time goes:
time: 106 us; the launch traced here: 105 us
  waiting for transfers between devices  39.3 us (37%)
  matrix products  22.3 us (21%)
  between operations  13.5 us (13%)
  blocking collectives  13.3 us (13%)
  starting transfers between devices  10.8 us (10%)
  local copies, waits for them, and re-layouts  3.83 us (4%)
  other arithmetic  2.29 us (2%)
    psum x1, waiting for transfers between devices, local(): full = lax.psum(partial_value, 'cuts')  30.2 us
    all_to_all x1, blocking collectives, local(): lax.all_to_all(stacked, 'elem', split_axis=2, concat_axis=0, tiled=True)  13.3 us
    dot_general x1, matrix products, local(): jnp.dot(projectors[0].reshape(groups * span, points), scaled, preferred_e...  12.2 us
    ppermute x4, starting transfers between devices, passed_along(): return lax.ppermute(block, axis, route)  10.8 us
    dot_general x7, matrix products, pair_block(): jnp.einsum('ib,ic->bc', left * weights[:, None], right, precision=lax.Pre...  9.95 us
    ppermute x4, waiting for transfers between devices, passed_along(): return lax.ppermute(block, axis, route)  9.06 us
  transfers between devices with their start and end apart: 5, of which 2 were waited for; matrix products, arithmetic and copies ran while one was open for 8% of the time, Pallas kernels for 0%

commit v1 on v0

--- a/solution.py
+++ b/solution.py
@@ -30,7 +30,7 @@
     table = jnp.dot(onehot, gamma_table, precision=lax.Precision.HIGHEST)
     active = (jnp.arange(slots, dtype=jnp.int32)[None, :] < counts[0][:, None]).astype(jnp.float32)
     energy = (table * active).reshape(span)
-    full = lax.psum(partial_value, "cuts")
+    full = jnp.sum(lax.all_gather(partial_value, axis_name="cuts"), axis=0)
     left_whole, left_energy = passed_along((full[span:], energy), "elem", 1)
     right_whole, right_energy = passed_along((full[: 2 * span], energy), "elem", -1)
     start = cut_index * quarter

time: 106 us -> 95 us (0.90)
  matrix products: 22.3 us -> 15.6 us
  waiting for transfers between devices: 39.3 us -> 36.8 us
  other arithmetic: 2.29 us -> 4.34 us
  blocking collectives: 13.3 us -> 11.6 us
  local copies, waits for them, and re-layouts: 3.83 us -> 2.65 us
    psum x1 -> x0, waiting for transfers between devices: 30.2 us -> none  [local(): full = lax.psum(partial_value, 'cuts')]
    all_gather x0 -> x1, waiting for transfers between devices: none -> 22 us  [local(): full = jnp.sum(lax.all_gather(partial_value, axis_name='cuts'), axis=0)]
    dot_general x7, matrix products: 9.95 us -> 3.21 us  [pair_block(): jnp.einsum('ib,ic->bc', left * weights[:, None], right, precision=lax.Pre...]
    ppermute x4, waiting for transfers between devices: 9.06 us -> 14.8 us  [passed_along(): return lax.ppermute(block, axis, route)]
    reduce_sum x0 -> x1, other arithmetic: none -> 2.05 us  [local(): full = jnp.sum(lax.all_gather(partial_value, axis_name='cuts'), axis=0)]
    all_to_all x1, blocking collectives: 13.3 us -> 11.6 us  [local(): lax.all_to_all(stacked, 'elem', split_axis=2, concat_axis=0, tiled=True)]
    slice x1, local copies, waits for them, and re-layouts: 1.35 us -> 0.17 us  [local(): left_whole, left_energy = passed_along((full[span:], energy), 'elem', 1)]
  transfers between devices with their start and end apart: 5 -> 5, of which waited for: 2 -> 2; matrix products, arithmetic and copies ran while one was open for 8% -> 5% of each run, Pallas kernels for 0% -> 0%
where the time goes in v1:
time: 95 us; the launch traced here: 94.8 us
  waiting for transfers between devices  36.8 us (39%)
  matrix products  15.6 us (16%)
  between operations  13.5 us (14%)
  blocking collectives  11.6 us (12%)
  starting transfers between devices  10.3 us (11%)
  other arithmetic  4.34 us (5%)
  local copies, waits for them, and re-layouts  2.65 us (3%)
    all_gather x1, waiting for transfers between devices, local(): full = jnp.sum(lax.all_gather(partial_value, axis_name='cuts'), axis=0)  22 us
    ppermute x4, waiting for transfers between devices, passed_along(): return lax.ppermute(block, axis, route)  14.8 us
    dot_general x1, matrix products, local(): jnp.dot(projectors[0].reshape(groups * span, points), scaled, preferred_e...  12.2 us
    all_to_all x1, blocking collectives, local(): lax.all_to_all(stacked, 'elem', split_axis=2, concat_axis=0, tiled=True)  11.6 us
    ppermute x4, starting transfers between devices, passed_along(): return lax.ppermute(block, axis, route)  10.3 us
    dot_general x7, matrix products, pair_block(): jnp.einsum('ib,ic->bc', left * weights[:, None], right, precision=lax.Pre...  3.21 us
    reduce_sum x1, other arithmetic, local(): full = jnp.sum(lax.all_gather(partial_value, axis_name='cuts'), axis=0)  2.05 us
  transfers between devices with their start and end apart: 5, of which 2 were waited for; matrix products, arithmetic and copies ran while one was open for 5% of the time, Pallas kernels for 0%

profile of v1, /device:TPU:0, one launch (start us, length us, event | category | flops | bytes accessed | tf_op | source)
XLA Modules:
  0.0 94.8 jit_solution(16200541368524280856)
XLA Ops:
  6.5 12.2 %fusion.4 = f32[1,960,160]{1,2,0:T(8,128)} fusion(bf16[960,8192]{1,0:T(8,128)(2,1)} %bitcast.34, bf16[1,8192,160]{1,2,0:T(8,128)(2,1)} %param.6, f32[8192]{0:T(1024)} %bitcast.35), kind=kOutput, calls=%fused_computation.4 | convolution fusion | flops 2520514560 | bytes 18997248 | tf_op jit(solution)/shard_map/dot_general | solution.py:24
  18.8 0.2 convolution_select_fusion
  19.1 6.0 %collective-permute-start.2 = (f32[320]{0:T(512)S(1)}, f32[320]{0:T(512)S(1)}, u32[]{:S(2)}, u32[]{:S(2)}) collective-permute-start(f32[320]{0:T(512)S(1)} %reshape.16), channel_id=1, source_target_pairs={{4,0},{8,4},{12,8},{16,12},{20,16},{24,20},{28,24},{0,28},{5,1},{9... | collective-permute-start | bytes 3848 | tf_op jit(solution)/shard_map/ppermute | solution.py:10
  25.1 22.0 %all-gather.4.cloned.1.call-done = f32[4,960,160]{1,2,0:T(8,128)} async-done(((f32[1,960,160]{1,2,0:T(8,128)}), f32[4,960,160]{1,2,0:T(8,128)}) %all-gather.4.cloned.1.call-update) | async-done | bytes 2457616 | tf_op jit(solution)/shard_map/all_gather | solution.py:33
  47.2 2.1 %reduce_sum.9 = f32[960,160]{0,1:T(8,128)S(1)} reduce(f32[4,960,160]{1,2,0:T(8,128)} %all-gather.4.cloned.1.call-done, f32[]{:T(128)} %constant.5.clone.1), dimensions={0}, to_apply=%region_0.0 | reduce | flops 460800 | bytes 3072004 | tf_op jit(solution)/shard_map/reduce_sum | solution.py:33
  49.2 0.2 fusion.33
  49.4 4.3 %collective-permute-start.3 = (f32[640,160]{0,1:T(8,128)S(1)}, f32[640,160]{0,1:T(8,128)S(1)}, u32[]{:S(2)}, u32[]{:S(2)}) collective-permute-start(f32[640,160]{0,1:T(8,128)S(1)} %get-tuple-element.6), channel_id=1, source_target_pairs={{4,0},{8,4},{12,8},{16,12},{20,16},{24,20},{28,24},{0,28},{5,1},{9... | collective-permute-start | bytes 1228808 | tf_op jit(solution)/shard_map/ppermute | solution.py:10
  53.7 0.5 fusion.13
  54.2 0.4 fusion.12
  54.6 0.4 fusion.10
  55.1 14.8 %collective-permute-done.3 = f32[640,160]{0,1:T(8,128)S(1)} collective-permute-done((f32[640,160]{0,1:T(8,128)S(1)}, f32[640,160]{0,1:T(8,128)S(1)}, u32[]{:S(2)}, u32[]{:S(2)}) %collective-permute-start.3) | collective-permute-done | bytes 409632 | tf_op jit(solution)/shard_map/ppermute | solution.py:10
  69.8 0.5 fusion.11
  70.3 0.5 fusion.7
  70.8 0.5 fusion.14
  71.3 0.4 fusion.8
  71.8 0.2 copy.19
  71.9 0.5 broadcast.11
  72.4 1.4 %reduce.1 = f32[160,3,40]{2,1,0:T(4,128)S(1)} reduce(f32[160,3,1,40]{3,2,1,0:T(1,128)S(1)} %bitcast.33, f32[]{:T(128)} %broadcast.11), dimensions={2}, to_apply=%bitcast.26.reduce_sub_computation | reduce | bytes 153604
  73.9 0.3 reshape.21
  74.2 11.6 %all_to_all.18 = f32[8,1,2400]{2,1,0:T(1,128)S(1)} all-to-all(f32[8,1,2400]{2,1,0:T(1,128)S(1)} %reshape.21), channel_id=1, replica_groups=mesh['elem'=8,'cuts'=4] {'elem'}, dimensions={0} | all-to-all | bytes 153600 | tf_op jit(solution)/shard_map/all_to_all | solution.py:54
  85.8 0.8 reduce.2
  86.6 0.5 reshape.22
  87.1 0.2 copy.20
  87.2 0.7 copy.23
  (16 shorter events, 0.2 us)
Async XLA Ops:
  6.5 12.2 %copy-start = (f32[4,16]{1,0:T(4,128)S(1)}, f32[4,16]{1,0:T(4,128)}, u32[]{:S(2)}) copy-start(f32[4,16]{1,0:T(4,128)} %param.11) | copy-start | bytes 772
  6.5 40.6 %all-gather.4.cloned.1.call-start = ((), (), s32[]{:S(2)}) async-start(), calls=%async_computation.1 | async-start | bytes 3276800 | tf_op jit(solution)/shard_map/all_gather | solution.py:33
  6.5 12.2 %copy-start.1 = (s32[1,20]{1,0:T(1,128)S(1)}, s32[1,20]{1,0:T(1,128)}, u32[]{:S(2)}) copy-start(s32[1,20]{1,0:T(1,128)} %param.9) | copy-start | bytes 244
  6.5 12.2 %copy-start.2 = (s32[1,20]{1,0:T(1,128)S(1)}, s32[1,20]{1,0:T(1,128)}, u32[]{:S(2)}) copy-start(s32[1,20]{1,0:T(1,128)} %param.10) | copy-start | bytes 244
  19.1 35.0 %collective-permute-start.2 = (f32[320]{0:T(512)S(1)}, f32[320]{0:T(512)S(1)}, u32[]{:S(2)}, u32[]{:S(2)}) collective-permute-start(f32[320]{0:T(512)S(1)} %reshape.16), channel_id=1, source_target_pairs={{4,0},{8,4},{12,8},{16,12},{20,16},{24,20},{28,24},{0,28},{5,1},{9... | collective-permute-start | bytes 3848 | tf_op jit(solution)/shard_map/ppermute | solution.py:10
  25.1 29.5 %collective-permute-start = (f32[320]{0:T(512)S(1)}, f32[320]{0:T(512)S(1)}, u32[]{:S(2)}, u32[]{:S(2)}) collective-permute-start(f32[320]{0:T(512)S(1)} %reshape.16), channel_id=1, source_target_pairs={{28,0},{0,4},{4,8},{8,12},{12,16},{16,20},{20,24},{24,28},{29,1},{... | collective-permute-start | bytes 3848 | tf_op jit(solution)/shard_map/ppermute | solution.py:10
  49.4 20.4 %collective-permute-start.3 = (f32[640,160]{0,1:T(8,128)S(1)}, f32[640,160]{0,1:T(8,128)S(1)}, u32[]{:S(2)}, u32[]{:S(2)}) collective-permute-start(f32[640,160]{0,1:T(8,128)S(1)} %get-tuple-element.6), channel_id=1, source_target_pairs={{4,0},{8,4},{12,8},{16,12},{20,16},{24,20},{28,24},{0,28},{5,1},{9... | collective-permute-start | bytes 1228808 | tf_op jit(solution)/shard_map/ppermute | solution.py:10
  53.7 17.1 %collective-permute-start.1 = (f32[640,160]{0,1:T(8,128)S(1)}, f32[640,160]{0,1:T(8,128)S(1)}, u32[]{:S(2)}, u32[]{:S(2)}) collective-permute-start(f32[640,160]{0,1:T(8,128)S(1)} %get-tuple-element.5), channel_id=1, source_target_pairs={{28,0},{0,4},{4,8},{8,12},{12,16},{16,20},{20,24},{24,28},{29,1},{... | collective-permute-start | bytes 1228808 | tf_op jit(solution)/shard_map/ppermute | solution.py:10
Sparse Core Ops, SparseCore 0:
  18.9 28.2 all-gather.3
